TPU v7x, 128 devices: a whole 4x4x4 slice. The times are simulated.
128 devices in a mesh: dof: 32 (over x, z, core), snap: 4 (over y).
Axes of the slice: x: 4, y: 4, z: 4, core: 2. Of those that a mesh axis runs over, the one named last changes fastest.
Arguments:
- snapshots: bfloat16 [131072, 1024], P('dof', 'snap')
- lengths: int32 [16], replicated, may hold values from 16 to 64, as said below
- start_block: float32 [1024, 128], replicated, may hold values from -6 to 6
Outputs:
- pod_modes: float32 [131072, 128], P(('dof', 'snap'))
- r_factor: float32 [1024, 1024], replicated
Inputs may be any that keep to these rules, and one draw needn't show every extreme that they name: `lengths`: some passage has all 64 steps active and some passage only a quarter of them.
All inputs are finite; a program needn't handle non-finite values.
Results may differ from a plain program's by a relative error of at most 0.0003.
Values may be sent and summed in bfloat16 or wider, within the bound.
No kernel may reach another device: no remote copies, remote signals or barrier semaphores. Data moves between devices by JAX's collectives and lax.ppermute only.
A program may use at most 128 MiB of HBM per device.

v0:
```python
import jax
import jax.numpy as jnp
from jax import lax
from jax.sharding import PartitionSpec as P

STEPS = 64
ITERS = 3
PASSES = 16


def body(snapshots, lengths, start_block):
    panel_width = snapshots.shape[1]
    first_col = lax.axis_index("snap") * panel_width
    columns = first_col + jnp.arange(panel_width, dtype=jnp.int32)
    passage = columns // STEPS
    lookup = passage[:, None] == jnp.arange(PASSES, dtype=jnp.int32)[None, :]
    col_length = jnp.sum(jnp.where(lookup, lengths[None, :], 0), axis=1)
    active = columns % STEPS < col_length
    masked = jnp.where(active[None, :], snapshots, jnp.zeros_like(snapshots))
    gathered_slab = lax.all_gather(masked, "snap", axis=1, tiled=True)
    row_count = gathered_slab.shape[0] * lax.axis_size("dof")
    contract = (((0,), (0,)), ((), ()))
    partial_gram = lax.dot_general(
        gathered_slab, gathered_slab, contract, preferred_element_type=jnp.float32
    )
    gram_sum = lax.psum(partial_gram, "dof")
    width = gram_sum.shape[0]
    shifted = gram_sum / jnp.float32(row_count) + 0.05 * jnp.eye(width, dtype=jnp.float32)
    upper_factor = jnp.linalg.cholesky(shifted).T
    subspace = start_block
    for sweep in range(ITERS):
        image = jnp.dot(
            shifted, subspace, precision=lax.Precision.HIGHEST, preferred_element_type=jnp.float32
        )
        correlation = lax.dot_general(
            image,
            image,
            contract,
            precision=lax.Precision.HIGHEST,
            preferred_element_type=jnp.float32,
        )
        lower_factor = jnp.linalg.cholesky(correlation)
        subspace = lax.linalg.triangular_solve(
            lower_factor, image, left_side=False, lower=True, transpose_a=True
        )
    quarter = gathered_slab.shape[0] // lax.axis_size("snap")
    own_rows = lax.dynamic_slice_in_dim(
        gathered_slab, lax.axis_index("snap") * quarter, quarter, 0
    ).astype(jnp.float32)
    pod_modes = jnp.dot(
        own_rows, subspace, precision=lax.Precision.HIGHEST, preferred_element_type=jnp.float32
    )
    return (pod_modes, upper_factor)


def solution(mesh):
    placed = (P("dof", "snap"), P(), P())
    return jax.shard_map(
        body, mesh=mesh, in_specs=placed, out_specs=(P(("dof", "snap"), None), P()), check_vma=False
    )
```

profile of v0, /device:TPU:1, one launch (start us, length us, event | category | flops | bytes accessed | tf_op | source)
XLA Modules:
  0.0 570.0 jit_solution(12406197987237153935)
XLA Ops:
  11.2 89.9 %all-gather.2.cloned.1.call-done = bf16[4096,1024]{1,0:T(8,128)(2,1)} async-done(((bf16[4096,256]{1,0:T(8,128)(2,1)}), bf16[4096,1024]{1,0:T(8,128)(2,1)}) %all-gather.2.cloned.1.call-update) | async-done | bytes 8388624 | tf_op jit(solution)/shard_map/all_gather | solution.py:20
  101.0 15.0 %fusion.79 = f32[1024,1024]{0,1:T(8,128)} fusion(bf16[4096,1024]{1,0:T(8,128)(2,1)} %all-gather.2.cloned.1.call-done), kind=kOutput, calls=%fused_computation.138 | convolution fusion | flops 8589934592 | bytes 12582912 | tf_op jit(solution)/shard_map/dot_general | solution.py:23
  116.1 113.1 %all-reduce.3.cloned.1.call-done = f32[1024,1024]{0,1:T(8,128)} async-done(((f32[1024,1024]{0,1:T(8,128)}), f32[1024,1024]{0,1:T(8,128)}) %all-reduce.3.cloned.1.call-update) | async-done | bytes 4194320 | tf_op jit(solution)/shard_map/psum | solution.py:26
  229.2 5.1 select_add_fusion
  234.3 5.8 %copy.29 = f32[1024,1024]{1,0:T(8,128)} copy(f32[1024,1024]{0,1:T(8,128)} %select_add_fusion) | data formatting | bytes 8388608 | tf_op jit(solution)/shard_map/add | solution.py:28
  240.1 4.5 fusion
  246.6 11.7 %cholesky.247 = f32[128,128]{1,0:T(8,128)S(1)} custom-call(f32[128,128]{1,0:T(8,128)S(1)} %cholesky.667), custom_call_target="Cholesky" | custom-call | tf_op jit(solution)/shard_map/jit(cholesky)/cholesky | solution.py:29
  258.5 9.8 %custom-call.64 = f32[1,128,128]{1,2,0:T(8,128)S(1)} custom-call(f32[1,128,128]{2,1,0:T(8,128)S(1)} %get-tuple-element.17), custom_call_target="InvertDiagBlocksLowerTriangular" | custom-call | tf_op jit(solution)/shard_map/jit(cholesky)/cholesky | solution.py:29
  271.6 11.7 %cholesky.270 = f32[128,128]{1,0:T(8,128)S(1)} custom-call(f32[128,128]{1,0:T(8,128)S(1)} %cholesky.671), custom_call_target="Cholesky" | custom-call | tf_op jit(solution)/shard_map/jit(cholesky)/cholesky | solution.py:29
  283.6 9.8 %custom-call.65 = f32[1,128,128]{1,2,0:T(8,128)S(1)} custom-call(f32[1,128,128]{2,1,0:T(8,128)S(1)} %get-tuple-element.15), custom_call_target="InvertDiagBlocksLowerTriangular" | custom-call | tf_op jit(solution)/shard_map/jit(cholesky)/cholesky | solution.py:29
  298.9 11.7 %cholesky.493 = f32[128,128]{1,0:T(8,128)S(1)} custom-call(f32[128,128]{1,0:T(8,128)S(1)} %cholesky.676), custom_call_target="Cholesky" | custom-call | tf_op jit(solution)/shard_map/jit(cholesky)/cholesky | solution.py:29
  311.4 9.8 %custom-call.66 = f32[1,128,128]{1,2,0:T(8,128)S(1)} custom-call(f32[1,128,128]{2,1,0:T(8,128)S(1)} %get-tuple-element.13), custom_call_target="InvertDiagBlocksLowerTriangular" | custom-call | tf_op jit(solution)/shard_map/jit(cholesky)/cholesky | solution.py:29
  325.8 11.7 %cholesky.512 = f32[128,128]{1,0:T(8,128)S(1)} custom-call(f32[128,128]{1,0:T(8,128)S(1)} %cholesky.681), custom_call_target="Cholesky" | custom-call | tf_op jit(solution)/shard_map/jit(cholesky)/cholesky | solution.py:29
  338.3 9.8 %custom-call.67 = f32[1,128,128]{1,2,0:T(8,128)S(1)} custom-call(f32[1,128,128]{2,1,0:T(8,128)S(1)} %get-tuple-element.11), custom_call_target="InvertDiagBlocksLowerTriangular" | custom-call | tf_op jit(solution)/shard_map/jit(cholesky)/cholesky | solution.py:29
  352.4 12.1 %cholesky.531 = f32[128,128]{1,0:T(8,128)S(1)} custom-call(f32[128,128]{1,0:T(8,128)S(1)} %cholesky.686), custom_call_target="Cholesky" | custom-call | tf_op jit(solution)/shard_map/jit(cholesky)/cholesky | solution.py:29
  365.3 9.8 %custom-call.68 = f32[1,128,128]{1,2,0:T(8,128)S(1)} custom-call(f32[1,128,128]{2,1,0:T(8,128)S(1)} %get-tuple-element.9), custom_call_target="InvertDiagBlocksLowerTriangular" | custom-call | tf_op jit(solution)/shard_map/jit(cholesky)/cholesky | solution.py:29
  379.4 11.7 %cholesky.551 = f32[128,128]{1,0:T(8,128)S(1)} custom-call(f32[128,128]{1,0:T(8,128)S(1)} %cholesky.691), custom_call_target="Cholesky" | custom-call | tf_op jit(solution)/shard_map/jit(cholesky)/cholesky | solution.py:29
  391.9 9.8 %custom-call.69 = f32[1,128,128]{1,2,0:T(8,128)S(1)} custom-call(f32[1,128,128]{2,1,0:T(8,128)S(1)} %get-tuple-element.7), custom_call_target="InvertDiagBlocksLowerTriangular" | custom-call | tf_op jit(solution)/shard_map/jit(cholesky)/cholesky | solution.py:29
  405.5 11.7 %cholesky.571 = f32[128,128]{1,0:T(8,128)S(1)} custom-call(f32[128,128]{1,0:T(8,128)S(1)} %cholesky.696), custom_call_target="Cholesky" | custom-call | tf_op jit(solution)/shard_map/jit(cholesky)/cholesky | solution.py:29
  418.0 9.8 %custom-call.70 = f32[1,128,128]{1,2,0:T(8,128)S(1)} custom-call(f32[1,128,128]{2,1,0:T(8,128)S(1)} %get-tuple-element.5), custom_call_target="InvertDiagBlocksLowerTriangular" | custom-call | tf_op jit(solution)/shard_map/jit(cholesky)/cholesky | solution.py:29
  430.9 11.7 %cholesky.589 = f32[128,128]{1,0:T(8,128)S(1)} custom-call(f32[128,128]{1,0:T(8,128)S(1)} %convolution_subtract_fusion.6), custom_call_target="Cholesky" | custom-call | tf_op jit(solution)/shard_map/jit(cholesky)/cholesky | solution.py:29
  442.7 9.0 %fusion.78 = f32[1024,128]{1,0:T(8,128)S(1)} fusion(f32[1024,128]{1,0:T(8,128)S(1)} %copy-done, f32[1024,1024]{0,1:T(8,128)} %all-reduce.3.cloned.1.call-done), kind=kOutput, calls=%fused_computation.137 | convolution fusion | flops 1614807040 | bytes 5242880 | tf_op jit(solution)/shard_map/dot_general | solution.py:32
  452.9 11.7 %cholesky.636 = f32[128,128]{1,0:T(8,128)S(1)} custom-call(f32[128,128]{1,0:T(8,128)S(1)} %fusion.38), custom_call_target="Cholesky" | custom-call | tf_op jit(solution)/shard_map/jit(cholesky)/cholesky | solution.py:42
  465.9 9.8 %custom-call.73 = f32[1,128,128]{1,2,0:T(8,128)S(1)} custom-call(f32[1,128,128]{2,1,0:T(8,128)S(1)} %fusion.21), custom_call_target="InvertDiagBlocksLowerTriangular" | custom-call | tf_op jit(solution)/shard_map/triangular_solve/custom-call.16 | solution.py:43
  476.4 9.2 %fusion.77 = f32[1024,128]{1,0:T(8,128)S(1)} fusion(f32[1024,128]{0,1:T(8,128)S(1)} %convolution_bitcast_fusion.2, f32[1024,1024]{0,1:T(8,128)} %all-reduce.3.cloned.1.call-done), kind=kOutput, calls=%fused_computation.136 | convolution fusion | flops 1614807040 | bytes 5242880 | tf_op jit(solution)/shard_map/dot_general | solution.py:32
  486.7 11.7 %cholesky.647 = f32[128,128]{1,0:T(8,128)S(1)} custom-call(f32[128,128]{1,0:T(8,128)S(1)} %fusion.36), custom_call_target="Cholesky" | custom-call | tf_op jit(solution)/shard_map/jit(cholesky)/cholesky | solution.py:42
  499.8 9.8 %custom-call.74 = f32[1,128,128]{1,2,0:T(8,128)S(1)} custom-call(f32[1,128,128]{2,1,0:T(8,128)S(1)} %fusion.22), custom_call_target="InvertDiagBlocksLowerTriangular" | custom-call | tf_op jit(solution)/shard_map/triangular_solve/custom-call.16 | solution.py:43
  510.3 9.0 %fusion.76 = f32[1024,128]{1,0:T(8,128)S(1)} fusion(f32[1024,128]{0,1:T(8,128)S(1)} %convolution_bitcast_fusion.1, f32[1024,1024]{0,1:T(8,128)} %all-reduce.3.cloned.1.call-done), kind=kOutput, calls=%fused_computation.135 | convolution fusion | flops 1614807040 | bytes 5242880 | tf_op jit(solution)/shard_map/dot_general | solution.py:32
  520.3 11.7 %cholesky.658 = f32[128,128]{1,0:T(8,128)S(1)} custom-call(f32[128,128]{1,0:T(8,128)S(1)} %fusion.34), custom_call_target="Cholesky" | custom-call | tf_op jit(solution)/shard_map/jit(cholesky)/cholesky | solution.py:42
  533.4 9.8 %custom-call.75 = f32[1,128,128]{1,2,0:T(8,128)S(1)} custom-call(f32[1,128,128]{2,1,0:T(8,128)S(1)} %fusion.23), custom_call_target="InvertDiagBlocksLowerTriangular" | custom-call | tf_op jit(solution)/shard_map/triangular_solve/custom-call.16 | solution.py:43
  553.9 4.9 select_bitcast_fusion
  558.8 4.2 fusion.1
  (89 shorter events, 53.5 us)
Async XLA Ops:
  7.2 435.6 %copy-start = (f32[1024,128]{1,0:T(8,128)S(1)}, f32[1024,128]{1,0:T(8,128)}, u32[]{:S(2)}) copy-start(f32[1024,128]{1,0:T(8,128)} %param.8) | copy-start | bytes 1572868
  7.2 93.9 %all-gather.2.cloned.1.call-start = ((), (), s32[]{:S(2)}) async-start(), calls=%async_computation | async-start | bytes 10485760 | tf_op jit(solution)/shard_map/all_gather | solution.py:20
  11.1 218.1 %all-reduce.3.cloned.1.call-start = ((), (), s32[]{:S(2)}) async-start(), calls=%async_computation.1 | async-start | bytes 8388608 | tf_op jit(solution)/shard_map/psum | solution.py:26
  244.6 2.0 copy-start.2
  294.5 2.0 copy-start.1
Sparse Core Ops, SparseCore 0:
  11.2 89.7 all-gather.1
  116.2 112.9 all-reduce.2
where the time goes:
time: 575 us; the launch traced here: 570 us
  other arithmetic  254 us (44%)
  waiting for transfers between devices  203 us (35%)
  matrix products  77.3 us (13%)
  between operations  19.6 us (3%)
  local copies, waits for them, and re-layouts  15.6 us (3%)
    another operation x30, other arithmetic, body(): upper_factor = jnp.linalg.cholesky(shifted).T  167 us
    psum x1, waiting for transfers between devices, body(): gram_sum = lax.psum(partial_gram, 'dof')  113 us
    all_gather x1, waiting for transfers between devices, body(): gathered_slab = lax.all_gather(masked, 'snap', axis=1, tiled=True)  89.9 us
    another operation x9, other arithmetic, body(): lower_factor = jnp.linalg.cholesky(correlation)  37.2 us
    another operation x6, other arithmetic, body(): lax.linalg.triangular_solve(lower_factor, image, left_side=False, lower=T...  31.4 us
    dot_general x3, matrix products, body(): jnp.dot(shifted, subspace, precision=lax.Precision.HIGHEST, preferred_ele...  27.2 us
    another operation x14, matrix products, body(): upper_factor = jnp.linalg.cholesky(shifted).T  25.9 us
    dot_general x1, matrix products, body(): lax.dot_general(gathered_slab, gathered_slab, contract, preferred_element...  15 us
  transfers between devices with their start and end apart: 2, of which 2 were waited for; matrix products, arithmetic and copies ran while one was open for 0% of the time, Pallas kernels for 0%

commit v1 on v0

v1 whole, which is shorter than its diff:
```python
import jax
import jax.numpy as jnp
from jax import lax
from jax.sharding import PartitionSpec as P

STEPS = 64
ITERS = 3
PASSES = 16
TILE = 128


def pack_upper(rows):
    width = rows.shape[1]
    pieces = []
    for i in range(width // TILE):
        lhs = rows[:, i * TILE:(i + 1) * TILE]
        rhs = rows[:, i * TILE:]
        pieces.append(
            lax.dot_general(lhs, rhs, (((0,), (0,)), ((), ())), preferred_element_type=jnp.float32)
        )
    return jnp.concatenate(pieces, axis=1)


def unpack_upper(packed, width):
    blocks = width // TILE
    upper_rows = []
    offset = 0
    for i in range(blocks):
        w = width - i * TILE
        piece = packed[:, offset:offset + w]
        offset += w
        upper_rows.append(jnp.pad(piece, ((0, 0), (i * TILE, 0))))
    upper = jnp.concatenate(upper_rows, axis=0)
    r = lax.broadcasted_iota(jnp.int32, (width, width), 0) // TILE
    c = lax.broadcasted_iota(jnp.int32, (width, width), 1) // TILE
    return jnp.where(r <= c, upper, upper.T)


def body(snapshots, lengths, start_block):
    rows = lax.all_to_all(snapshots, "snap", 0, 1, tiled=True)
    width = rows.shape[1]
    col_length = jnp.repeat(lengths, STEPS, total_repeat_length=width)
    columns = jnp.arange(width, dtype=jnp.int32)
    active = columns % STEPS < col_length
    masked = jnp.where(active[None, :], rows, jnp.zeros_like(rows))
    row_count = snapshots.shape[0] * lax.axis_size("dof")
    packed = lax.psum(pack_upper(masked), ("dof", "snap"))
    gram_sum = unpack_upper(packed, width)
    shifted = gram_sum / jnp.float32(row_count) + 0.05 * jnp.eye(width, dtype=jnp.float32)
    upper_factor = lax.linalg.cholesky(shifted, symmetrize_input=False).T
    contract = (((0,), (0,)), ((), ()))
    subspace = start_block
    for sweep in range(ITERS):
        image = jnp.dot(
            shifted, subspace, precision=lax.Precision.HIGHEST, preferred_element_type=jnp.float32
        )
        correlation = lax.dot_general(
            image, image, contract, precision=lax.Precision.HIGHEST, preferred_element_type=jnp.float32
        )
        lower_factor = jnp.linalg.cholesky(correlation)
        subspace = lax.linalg.triangular_solve(
            lower_factor, image, left_side=False, lower=True, transpose_a=True
        )
    pod_modes = jnp.dot(
        masked.astype(jnp.float32), subspace, precision=lax.Precision.HIGHEST,
        preferred_element_type=jnp.float32,
    )
    return (pod_modes, upper_factor)


def solution(mesh):
    placed = (P("dof", "snap"), P(), P())
    return jax.shard_map(
        body, mesh=mesh, in_specs=placed, out_specs=(P(("dof", "snap"), None), P()), check_vma=False
    )
```

time: 575 us -> 549 us (0.955)
  waiting for transfers between devices: 203 us -> 167 us
  matrix products: 77.3 us -> 57.1 us
  local copies, waits for them, and re-layouts: 15.6 us -> 28.4 us
  other arithmetic: 254 us -> 263 us
    all_gather x1 -> x0, waiting for transfers between devices: 89.9 us -> none  [body(): gathered_slab = lax.all_gather(masked, 'snap', axis=1, tiled=True)]
    psum x1, waiting for transfers between devices: 113 us -> 153 us  [body(): packed = lax.psum(pack_upper(masked), ('dof', 'snap'))]
    all_to_all x0 -> x1, waiting for transfers between devices: none -> 14.4 us  [body(): rows = lax.all_to_all(snapshots, 'snap', 0, 1, tiled=True)]
    dot_general x3, matrix products: 27.2 us -> 16.5 us  [body(): jnp.dot(shifted, subspace, precision=lax.Precision.HIGHEST, preferred_ele...]
    unnamed x6 -> x16, local copies, waits for them, and re-layouts: 3.97 us -> 14.2 us
    dot_general x2 -> x9, matrix products: 19.2 us -> 12.6 us  [the longest x8 9.46 us: pack_upper(): lax.dot_general(lhs, rhs, (((0,), (0,)), ((), ())), preferred_element_typ...]
    concatenate x0 -> x2, local copies, waits for them, and re-layouts: none -> 6.18 us  [unpack_upper(): upper = jnp.concatenate(upper_rows, axis=0)]
    add x1 -> x0, local copies, waits for them, and re-layouts: 5.81 us -> none  [body(): gram_sum / jnp.float32(row_count) + 0.05 * jnp.eye(width, dtype=jnp.float32)]
  transfers between devices with their start and end apart: 2 -> 2, of which waited for: 2 -> 2; matrix products, arithmetic and copies ran while one was open for 0% -> 2% of each run, Pallas kernels for 0% -> 0%
where the time goes in v1:
time: 549 us; the launch traced here: 541 us
  other arithmetic  263 us (48%)
  waiting for transfers between devices  167 us (30%)
  matrix products  57.1 us (10%)
  local copies, waits for them, and re-layouts  28.4 us (5%)
  between operations  19.9 us (4%)
    another operation x31, other arithmetic, body(): upper_factor = lax.linalg.cholesky(shifted, symmetrize_input=False).T  173 us
    psum x1, waiting for transfers between devices, body(): packed = lax.psum(pack_upper(masked), ('dof', 'snap'))  153 us
    another operation x9, other arithmetic, body(): lower_factor = jnp.linalg.cholesky(correlation)  37.2 us
    another operation x6, other arithmetic, body(): lax.linalg.triangular_solve(lower_factor, image, left_side=False, lower=T...  31.4 us
    another operation x14, matrix products, body(): upper_factor = lax.linalg.cholesky(shifted, symmetrize_input=False).T  23.1 us
    dot_general x3, matrix products, body(): jnp.dot(shifted, subspace, precision=lax.Precision.HIGHEST, preferred_ele...  16.5 us
    all_to_all x1, waiting for transfers between devices, body(): rows = lax.all_to_all(snapshots, 'snap', 0, 1, tiled=True)  14.4 us
    unnamed x16, local copies, waits for them, and re-layouts  14.2 us
  transfers between devices with their start and end apart: 2, of which 2 were waited for; matrix products, arithmetic and copies ran while one was open for 2% of the time, Pallas kernels for 0%

profile of v1, /device:TPU:1, one launch (start us, length us, event | category | flops | bytes accessed | tf_op | source)
XLA Modules:
  0.0 540.6 jit_solution(2373709611297239090)
XLA Ops:
  7.2 5.2 all-to-all-start
  13.2 4.4 compare_select_fusion.1
  17.7 5.7 %fusion.98 = pred[1024]{0:T(1024)(128)(4,1)S(1)} fusion(pred[1024]{0:T(1024)(128)(4,1)S(1)} %get-tuple-element.30, pred[1024]{0:T(1024)(128)(4,1)S(1)} %get-tuple-element.29, pred[1024]{0:T(1024)(128)(4,1)S(1)} %get-tuple-element.28, pred[1024]{0:T(1024)(128)(4,1)S(1)} %get-tuple-element.27, pred[1024]{0:T(1024)(128)(4,1)S(1)} %get-tuple-element.26, ...), kind=kLoop, calls=%fused_computation.159 | loop fusion | flops 25600 | bytes 18500 | tf_op jit(solution)/shard_map/lt | solution.py:44
  23.4 14.4 %all-to-all-done = bf16[4,1024,256]{2,1,0:T(8,128)(2,1)S(1)} async-done(((bf16[4,1024,256]{2,1,0:T(8,128)(2,1)}), bf16[4,1024,256]{2,1,0:T(8,128)(2,1)S(1)}, u32[]{:S(2)}, u32[]{:S(2)}) %all-to-all-start) | async-done | bytes 2097184 | tf_op jit(solution)/shard_map/all_to_all | solution.py:40
  51.5 152.7 %all-reduce.10.cloned.1.call-done = f32[128,4608]{0,1:T(8,128)} async-done(((f32[128,4608]{0,1:T(8,128)}), f32[128,4608]{0,1:T(8,128)}) %all-reduce.10.cloned.1.call-update) | async-done | bytes 2359312 | tf_op jit(solution)/shard_map/psum | solution.py:47
  214.1 5.3 copy.37
  225.7 11.7 %cholesky.247 = f32[128,128]{1,0:T(8,128)S(1)} custom-call(f32[128,128]{1,0:T(8,128)S(1)} %cholesky.667), custom_call_target="Cholesky" | custom-call | tf_op jit(solution)/shard_map/cholesky | solution.py:50
  238.1 9.8 %custom-call.49 = f32[1,128,128]{1,2,0:T(8,128)S(1)} custom-call(f32[1,128,128]{2,1,0:T(8,128)S(1)} %get-tuple-element.54), custom_call_target="InvertDiagBlocksLowerTriangular" | custom-call | tf_op jit(solution)/shard_map/cholesky | solution.py:50
  247.9 5.7 %fusion.106 = f32[1024,128]{1,0:T(8,128)S(1)} fusion(f32[1024,1024]{1,0:T(8,128)} %copy-done.1, f32[1024,128]{1,0:T(8,128)S(1)} %copy-done), kind=kOutput, calls=%fused_computation.190 | convolution fusion | flops 1610612736 | bytes 5242880 | tf_op jit(solution)/shard_map/dot_general | solution.py:54
  254.7 11.7 %cholesky.636 = f32[128,128]{1,0:T(8,128)S(1)} custom-call(f32[128,128]{1,0:T(8,128)S(1)} %fusion.63), custom_call_target="Cholesky" | custom-call | tf_op jit(solution)/shard_map/jit(cholesky)/cholesky | solution.py:60
  267.8 9.8 %custom-call.58 = f32[1,128,128]{1,2,0:T(8,128)S(1)} custom-call(f32[1,128,128]{2,1,0:T(8,128)S(1)} %fusion.46), custom_call_target="InvertDiagBlocksLowerTriangular" | custom-call | tf_op jit(solution)/shard_map/triangular_solve/custom-call.16 | solution.py:61
  278.2 5.4 fusion.108
  284.7 11.7 %cholesky.647 = f32[128,128]{1,0:T(8,128)S(1)} custom-call(f32[128,128]{1,0:T(8,128)S(1)} %fusion.61), custom_call_target="Cholesky" | custom-call | tf_op jit(solution)/shard_map/jit(cholesky)/cholesky | solution.py:60
  297.8 9.8 %custom-call.59 = f32[1,128,128]{1,2,0:T(8,128)S(1)} custom-call(f32[1,128,128]{2,1,0:T(8,128)S(1)} %fusion.47), custom_call_target="InvertDiagBlocksLowerTriangular" | custom-call | tf_op jit(solution)/shard_map/triangular_solve/custom-call.16 | solution.py:61
  308.3 5.4 %fusion.110 = f32[1024,128]{1,0:T(8,128)S(1)} fusion(f32[1024,1024]{1,0:T(8,128)} %copy-done.1, f32[1024,128]{0,1:T(8,128)S(1)} %convolution_bitcast_fusion.1), kind=kOutput, calls=%fused_computation.194 | convolution fusion | flops 1610612736 | bytes 5242880 | tf_op jit(solution)/shard_map/dot_general | solution.py:54
  314.8 11.7 %cholesky.658 = f32[128,128]{1,0:T(8,128)S(1)} custom-call(f32[128,128]{1,0:T(8,128)S(1)} %fusion.59), custom_call_target="Cholesky" | custom-call | tf_op jit(solution)/shard_map/jit(cholesky)/cholesky | solution.py:60
  327.9 9.8 %custom-call.60 = f32[1,128,128]{1,2,0:T(8,128)S(1)} custom-call(f32[1,128,128]{2,1,0:T(8,128)S(1)} %fusion.48), custom_call_target="InvertDiagBlocksLowerTriangular" | custom-call | tf_op jit(solution)/shard_map/triangular_solve/custom-call.16 | solution.py:61
  347.9 12.1 %cholesky.270 = f32[128,128]{1,0:T(8,128)S(1)} custom-call(f32[128,128]{1,0:T(8,128)S(1)} %cholesky.671), custom_call_target="Cholesky" | custom-call | tf_op jit(solution)/shard_map/cholesky | solution.py:50
  361.3 9.8 %custom-call.50 = f32[1,128,128]{1,2,0:T(8,128)S(1)} custom-call(f32[1,128,128]{2,1,0:T(8,128)S(1)} %get-tuple-element.51), custom_call_target="InvertDiagBlocksLowerTriangular" | custom-call | tf_op jit(solution)/shard_map/cholesky | solution.py:50
  374.5 11.7 %cholesky.493 = f32[128,128]{1,0:T(8,128)S(1)} custom-call(f32[128,128]{1,0:T(8,128)S(1)} %cholesky.676), custom_call_target="Cholesky" | custom-call | tf_op jit(solution)/shard_map/cholesky | solution.py:50
  387.6 10.0 %custom-call.51 = f32[1,128,128]{1,2,0:T(8,128)S(1)} custom-call(f32[1,128,128]{2,1,0:T(8,128)S(1)} %get-tuple-element.48), custom_call_target="InvertDiagBlocksLowerTriangular" | custom-call | tf_op jit(solution)/shard_map/cholesky | solution.py:50
  401.1 11.7 %cholesky.512 = f32[128,128]{1,0:T(8,128)S(1)} custom-call(f32[128,128]{1,0:T(8,128)S(1)} %cholesky.681), custom_call_target="Cholesky" | custom-call | tf_op jit(solution)/shard_map/cholesky | solution.py:50
  414.1 9.8 %custom-call.52 = f32[1,128,128]{1,2,0:T(8,128)S(1)} custom-call(f32[1,128,128]{2,1,0:T(8,128)S(1)} %get-tuple-element.45), custom_call_target="InvertDiagBlocksLowerTriangular" | custom-call | tf_op jit(solution)/shard_map/cholesky | solution.py:50
  427.3 11.9 %cholesky.531 = f32[128,128]{1,0:T(8,128)S(1)} custom-call(f32[128,128]{1,0:T(8,128)S(1)} %cholesky.686), custom_call_target="Cholesky" | custom-call | tf_op jit(solution)/shard_map/cholesky | solution.py:50
  440.5 9.8 %custom-call.53 = f32[1,128,128]{1,2,0:T(8,128)S(1)} custom-call(f32[1,128,128]{2,1,0:T(8,128)S(1)} %get-tuple-element.42), custom_call_target="InvertDiagBlocksLowerTriangular" | custom-call | tf_op jit(solution)/shard_map/cholesky | solution.py:50
  453.6 11.7 %cholesky.551 = f32[128,128]{1,0:T(8,128)S(1)} custom-call(f32[128,128]{1,0:T(8,128)S(1)} %cholesky.691), custom_call_target="Cholesky" | custom-call | tf_op jit(solution)/shard_map/cholesky | solution.py:50
  466.7 9.8 %custom-call.54 = f32[1,128,128]{1,2,0:T(8,128)S(1)} custom-call(f32[1,128,128]{2,1,0:T(8,128)S(1)} %get-tuple-element.39), custom_call_target="InvertDiagBlocksLowerTriangular" | custom-call | tf_op jit(solution)/shard_map/cholesky | solution.py:50
  479.5 11.9 %cholesky.571 = f32[128,128]{1,0:T(8,128)S(1)} custom-call(f32[128,128]{1,0:T(8,128)S(1)} %cholesky.696), custom_call_target="Cholesky" | custom-call | tf_op jit(solution)/shard_map/cholesky | solution.py:50
  492.7 9.8 %custom-call.55 = f32[1,128,128]{1,2,0:T(8,128)S(1)} custom-call(f32[1,128,128]{2,1,0:T(8,128)S(1)} %get-tuple-element.36), custom_call_target="InvertDiagBlocksLowerTriangular" | custom-call | tf_op jit(solution)/shard_map/cholesky | solution.py:50
  505.2 11.7 %cholesky.589 = f32[128,128]{1,0:T(8,128)S(1)} custom-call(f32[128,128]{1,0:T(8,128)S(1)} %convolution_subtract_fusion.6), custom_call_target="Cholesky" | custom-call | tf_op jit(solution)/shard_map/cholesky | solution.py:50
  523.1 4.8 select_bitcast_fusion
  528.0 5.3 copy.41
  (107 shorter events, 78.5 us)
Async XLA Ops:
  7.2 240.7 %copy-start = (f32[1024,128]{1,0:T(8,128)S(1)}, f32[1024,128]{1,0:T(8,128)}, u32[]{:S(2)}) copy-start(f32[1024,128]{1,0:T(8,128)} %param.10) | copy-start | bytes 1572868
  7.2 5.9 %copy-start.3 = (s32[8,128]{1,0:T(8,128)S(1)}, s32[8,128]{1,0:T(8,128)}, u32[]{:S(2)}) copy-start(s32[8,128]{1,0:T(8,128)} %constant.336.clone.1) | copy-start | bytes 12292
  7.2 5.2 copy-start.2
  7.2 30.6 %all-to-all-start = ((bf16[4,1024,256]{2,1,0:T(8,128)(2,1)}), bf16[4,1024,256]{2,1,0:T(8,128)(2,1)S(1)}, u32[]{:S(2)}, u32[]{:S(2)}) async-start(bf16[4,1024,256]{2,1,0:T(8,128)(2,1)} %bitcast.129), calls=%async_computation | async-start | bytes 4194304 | tf_op jit(solution)/shard_map/all_to_all | solution.py:40
  12.4 191.8 %all-reduce.10.cloned.1.call-start = ((), (), s32[]{:S(2)}) async-start(), calls=%async_computation.1 | async-start | bytes 4718592 | tf_op jit(solution)/shard_map/psum | solution.py:47
  204.2 5.7 %slice-start = ((f32[128,4608]{0,1:T(8,128)}), f32[128,640]{0,1:T(8,128)S(1)}, s32[]{:S(2)}) async-start(f32[128,4608]{0,1:T(8,128)} %all-reduce.10.cloned.1.call-done), calls=%async_computation.2 | async-start | bytes 655360 | tf_op jit(solution)/shard_map/slice | solution.py:30
  204.2 6.6 %slice-start.1 = ((f32[128,4608]{0,1:T(8,128)}), f32[128,512]{0,1:T(8,128)S(1)}, s32[]{:S(2)}) async-start(f32[128,4608]{0,1:T(8,128)} %all-reduce.10.cloned.1.call-done), calls=%async_computation.3 | async-start | bytes 524288 | tf_op jit(solution)/shard_map/slice | solution.py:30
  204.2 7.4 %slice-start.2 = ((f32[128,4608]{0,1:T(8,128)}), f32[128,384]{0,1:T(8,128)S(1)}, s32[]{:S(2)}) async-start(f32[128,4608]{0,1:T(8,128)} %all-reduce.10.cloned.1.call-done), calls=%async_computation.4 | async-start | bytes 393216 | tf_op jit(solution)/shard_map/slice | solution.py:30
  205.3 7.1 %slice-start.3 = ((f32[128,4608]{0,1:T(8,128)}), f32[128,256]{0,1:T(8,128)S(1)}, s32[]{:S(2)}) async-start(f32[128,4608]{0,1:T(8,128)} %all-reduce.10.cloned.1.call-done), calls=%async_computation.5 | async-start | bytes 262144 | tf_op jit(solution)/shard_map/slice | solution.py:30
  205.3 7.9 %slice-start.4 = ((f32[128,4608]{0,1:T(8,128)}), f32[128,128]{0,1:T(8,128)S(1)}, s32[]{:S(2)}) async-start(f32[128,4608]{0,1:T(8,128)} %all-reduce.10.cloned.1.call-done), calls=%async_computation.6 | async-start | bytes 131072 | tf_op jit(solution)/shard_map/slice | solution.py:30
  223.6 2.0 copy-start.1
Sparse Core Ops, SparseCore 0:
  51.6 152.5 all-reduce.9

commit v2 on v1

--- a/solution.py
+++ b/solution.py
@@ -36,6 +36,13 @@
     return jnp.where(r <= c, upper, upper.T)
 
 
+def all_reduce_a2a(x, axes):
+    received = lax.all_to_all(x, axes, 0, 0, tiled=True)
+    total = jnp.sum(received, axis=0, keepdims=True)
+    spread = jnp.broadcast_to(total, x.shape)
+    return lax.all_to_all(spread, axes, 0, 0, tiled=True)
+
+
 def body(snapshots, lengths, start_block):
     rows = lax.all_to_all(snapshots, "snap", 0, 1, tiled=True)
     width = rows.shape[1]
@@ -44,7 +51,7 @@
     active = columns % STEPS < col_length
     masked = jnp.where(active[None, :], rows, jnp.zeros_like(rows))
     row_count = snapshots.shape[0] * lax.axis_size("dof")
-    packed = lax.psum(pack_upper(masked), ("dof", "snap"))
+    packed = all_reduce_a2a(pack_upper(masked), ("dof", "snap"))
     gram_sum = unpack_upper(packed, width)
     shifted = gram_sum / jnp.float32(row_count) + 0.05 * jnp.eye(width, dtype=jnp.float32)
     upper_factor = lax.linalg.cholesky(shifted, symmetrize_input=False).T

time: 549 us -> 478 us (0.87)
  waiting for transfers between devices: 167 us -> 47.8 us
  blocking collectives: 0 us -> 43.5 us
  local copies, waits for them, and re-layouts: 28.4 us -> 44.1 us
  between operations: 19.9 us -> 6.55 us
    psum x1 -> x0, waiting for transfers between devices: 153 us -> none  [body(): packed = lax.psum(pack_upper(masked), ('dof', 'snap'))]
    all_to_all x0 -> x1, blocking collectives: none -> 43.5 us  [all_reduce_a2a(): received = lax.all_to_all(x, axes, 0, 0, tiled=True)]
    all_to_all x0 -> x1, waiting for transfers between devices: none -> 33.4 us  [all_reduce_a2a(): return lax.all_to_all(spread, axes, 0, 0, tiled=True)]
    all_to_all x0 -> x2, local copies, waits for them, and re-layouts: none -> 8.58 us  [the longest x1 6.16 us: all_reduce_a2a(): return lax.all_to_all(spread, axes, 0, 0, tiled=True)]
where the time goes in v2:
time: 478 us; the launch traced here: 470 us
  other arithmetic  266 us (56%)
  matrix products  51.7 us (11%)
  waiting for transfers between devices  47.8 us (10%)
  local copies, waits for them, and re-layouts  44.1 us (9%)
  blocking collectives  43.5 us (9%)
  starting transfers between devices  10.2 us (2%)
  between operations  6.55 us (1%)
    another operation x31, other arithmetic, body(): upper_factor = lax.linalg.cholesky(shifted, symmetrize_input=False).T  173 us
    all_to_all x1, blocking collectives, all_reduce_a2a(): received = lax.all_to_all(x, axes, 0, 0, tiled=True)  43.5 us
    another operation x9, other arithmetic, body(): lower_factor = jnp.linalg.cholesky(correlation)  37.2 us
    all_to_all x1, waiting for transfers between devices, all_reduce_a2a(): return lax.all_to_all(spread, axes, 0, 0, tiled=True)  33.4 us
    another operation x6, other arithmetic, body(): lax.linalg.triangular_solve(lower_factor, image, left_side=False, lower=T...  31.4 us
    another operation x14, matrix products, body(): upper_factor = lax.linalg.cholesky(shifted, symmetrize_input=False).T  23.1 us
    dot_general x3, matrix products, body(): jnp.dot(shifted, subspace, precision=lax.Precision.HIGHEST, preferred_ele...  16.4 us
    all_to_all x1, waiting for transfers between devices, body(): rows = lax.all_to_all(snapshots, 'snap', 0, 1, tiled=True)  14.4 us
  transfers between devices with their start and end apart: 2, of which 2 were waited for; matrix products, arithmetic and copies ran while one was open for 2% of the time, Pallas kernels for 0%

profile of v2, /device:TPU:1, one launch (start us, length us, event | category | flops | bytes accessed | tf_op | source)
XLA Modules:
  0.0 469.8 jit_solution(9850209844678339756)
XLA Ops:
  0.7 5.2 %all-to-all-start = ((bf16[4,1024,256]{2,1,0:T(8,128)(2,1)}), bf16[4,1024,256]{2,1,0:T(8,128)(2,1)S(1)}, u32[]{:S(2)}, u32[]{:S(2)}) async-start(bf16[4,1024,256]{2,1,0:T(8,128)(2,1)} %bitcast.140), calls=%async_computation | async-start | bytes 4194304 | tf_op jit(solution)/shard_map/all_to_all | solution.py:47
  11.1 5.7 %fusion.98 = pred[1024]{0:T(1024)(128)(4,1)S(1)} fusion(pred[1024]{0:T(1024)(128)(4,1)S(1)} %get-tuple-element.32, pred[1024]{0:T(1024)(128)(4,1)S(1)} %get-tuple-element.31, pred[1024]{0:T(1024)(128)(4,1)S(1)} %get-tuple-element.30, pred[1024]{0:T(1024)(128)(4,1)S(1)} %get-tuple-element.29, pred[1024]{0:T(1024)(128)(4,1)S(1)} %get-tuple-element.28, ...), kind=kLoop, calls=%fused_computation.159 | loop fusion | flops 25600 | bytes 18500 | tf_op jit(solution)/shard_map/lt | solution.py:51
  16.9 14.4 %all-to-all-done = bf16[4,1024,256]{2,1,0:T(8,128)(2,1)S(1)} async-done(((bf16[4,1024,256]{2,1,0:T(8,128)(2,1)}), bf16[4,1024,256]{2,1,0:T(8,128)(2,1)S(1)}, u32[]{:S(2)}, u32[]{:S(2)}) %all-to-all-start) | async-done | bytes 2097184 | tf_op jit(solution)/shard_map/all_to_all | solution.py:47
  42.0 43.5 %all_to_all.37 = f32[128,1,4608]{2,1,0:T(1,128)} all-to-all(f32[128,1,4608]{2,1,0:T(1,128)S(1)} %copy.26), channel_id=1, replica_groups=mesh['dof'=32,'snap'=4] {'dof','snap'}, dimensions={0} | all-to-all | bytes 4718592 | tf_op jit(solution)/shard_map/all_to_all | solution.py:40
  96.2 33.4 %all-to-all-done.2 = f32[128,1,4608]{2,1,0:T(1,128)} async-done(((f32[128,1,4608]{2,1,0:T(1,128)}), f32[128,1,4608]{2,1,0:T(1,128)}, u32[]{:S(2)}, u32[]{:S(2)}) %all-to-all-start.2) | async-done | bytes 2359328 | tf_op jit(solution)/shard_map/all_to_all | solution.py:43
  129.7 6.2 %copy.27 = f32[128,1,4608]{0,2,1:T(8,128)} copy(f32[128,1,4608]{2,1,0:T(1,128)} %all-to-all-done.2) | data formatting | bytes 4718592 | tf_op jit(solution)/shard_map/all_to_all | solution.py:43
  150.2 5.3 %copy.28 = f32[1024,1024]{1,0:T(8,128)} copy(f32[1024,1024]{0,1:T(8,128)} %pad_dynamic-update-slice_fusion) | data formatting | bytes 8388608 | tf_op jit(solution)/shard_map/concatenate | solution.py:33
  161.8 11.7 %cholesky.247 = f32[128,128]{1,0:T(8,128)S(1)} custom-call(f32[128,128]{1,0:T(8,128)S(1)} %cholesky.667), custom_call_target="Cholesky" | custom-call | tf_op jit(solution)/shard_map/cholesky | solution.py:57
  176.7 9.8 %custom-call.49 = f32[1,128,128]{1,2,0:T(8,128)S(1)} custom-call(f32[1,128,128]{2,1,0:T(8,128)S(1)} %get-tuple-element.56), custom_call_target="InvertDiagBlocksLowerTriangular" | custom-call | tf_op jit(solution)/shard_map/cholesky | solution.py:57
  186.5 5.6 %fusion.106 = f32[1024,128]{1,0:T(8,128)S(1)} fusion(f32[1024,1024]{1,0:T(8,128)} %copy-done.1, f32[1024,128]{1,0:T(8,128)S(1)} %copy-done), kind=kOutput, calls=%fused_computation.190 | convolution fusion | flops 1610612736 | bytes 5242880 | tf_op jit(solution)/shard_map/dot_general | solution.py:61
  193.2 11.7 %cholesky.636 = f32[128,128]{1,0:T(8,128)S(1)} custom-call(f32[128,128]{1,0:T(8,128)S(1)} %fusion.63), custom_call_target="Cholesky" | custom-call | tf_op jit(solution)/shard_map/jit(cholesky)/cholesky | solution.py:67
  206.3 9.8 %custom-call.58 = f32[1,128,128]{1,2,0:T(8,128)S(1)} custom-call(f32[1,128,128]{2,1,0:T(8,128)S(1)} %fusion.46), custom_call_target="InvertDiagBlocksLowerTriangular" | custom-call | tf_op jit(solution)/shard_map/triangular_solve/custom-call.16 | solution.py:68
  216.7 5.4 %fusion.108 = f32[1024,128]{1,0:T(8,128)S(1)} fusion(f32[1024,1024]{1,0:T(8,128)} %copy-done.1, f32[1024,128]{0,1:T(8,128)S(1)} %convolution_bitcast_fusion.2), kind=kOutput, calls=%fused_computation.192 | convolution fusion | flops 1610612736 | bytes 5242880 | tf_op jit(solution)/shard_map/dot_general | solution.py:61
  223.3 11.7 %cholesky.647 = f32[128,128]{1,0:T(8,128)S(1)} custom-call(f32[128,128]{1,0:T(8,128)S(1)} %fusion.61), custom_call_target="Cholesky" | custom-call | tf_op jit(solution)/shard_map/jit(cholesky)/cholesky | solution.py:67
  236.3 9.8 %custom-call.59 = f32[1,128,128]{1,2,0:T(8,128)S(1)} custom-call(f32[1,128,128]{2,1,0:T(8,128)S(1)} %fusion.47), custom_call_target="InvertDiagBlocksLowerTriangular" | custom-call | tf_op jit(solution)/shard_map/triangular_solve/custom-call.16 | solution.py:68
  246.8 5.4 %fusion.110 = f32[1024,128]{1,0:T(8,128)S(1)} fusion(f32[1024,1024]{1,0:T(8,128)} %copy-done.1, f32[1024,128]{0,1:T(8,128)S(1)} %convolution_bitcast_fusion.1), kind=kOutput, calls=%fused_computation.194 | convolution fusion | flops 1610612736 | bytes 5242880 | tf_op jit(solution)/shard_map/dot_general | solution.py:61
  253.4 11.7 %cholesky.658 = f32[128,128]{1,0:T(8,128)S(1)} custom-call(f32[128,128]{1,0:T(8,128)S(1)} %fusion.59), custom_call_target="Cholesky" | custom-call | tf_op jit(solution)/shard_map/jit(cholesky)/cholesky | solution.py:67
  266.4 9.8 %custom-call.60 = f32[1,128,128]{1,2,0:T(8,128)S(1)} custom-call(f32[1,128,128]{2,1,0:T(8,128)S(1)} %fusion.48), custom_call_target="InvertDiagBlocksLowerTriangular" | custom-call | tf_op jit(solution)/shard_map/triangular_solve/custom-call.16 | solution.py:68
  284.0 12.1 %cholesky.270 = f32[128,128]{1,0:T(8,128)S(1)} custom-call(f32[128,128]{1,0:T(8,128)S(1)} %cholesky.671), custom_call_target="Cholesky" | custom-call | tf_op jit(solution)/shard_map/cholesky | solution.py:57
  297.4 9.8 %custom-call.50 = f32[1,128,128]{1,2,0:T(8,128)S(1)} custom-call(f32[1,128,128]{2,1,0:T(8,128)S(1)} %get-tuple-element.53), custom_call_target="InvertDiagBlocksLowerTriangular" | custom-call | tf_op jit(solution)/shard_map/cholesky | solution.py:57
  310.6 11.7 %cholesky.493 = f32[128,128]{1,0:T(8,128)S(1)} custom-call(f32[128,128]{1,0:T(8,128)S(1)} %cholesky.676), custom_call_target="Cholesky" | custom-call | tf_op jit(solution)/shard_map/cholesky | solution.py:57
  323.7 10.0 %custom-call.51 = f32[1,128,128]{1,2,0:T(8,128)S(1)} custom-call(f32[1,128,128]{2,1,0:T(8,128)S(1)} %get-tuple-element.50), custom_call_target="InvertDiagBlocksLowerTriangular" | custom-call | tf_op jit(solution)/shard_map/cholesky | solution.py:57
  337.1 11.7 %cholesky.512 = f32[128,128]{1,0:T(8,128)S(1)} custom-call(f32[128,128]{1,0:T(8,128)S(1)} %cholesky.681), custom_call_target="Cholesky" | custom-call | tf_op jit(solution)/shard_map/cholesky | solution.py:57
  350.1 9.8 %custom-call.52 = f32[1,128,128]{1,2,0:T(8,128)S(1)} custom-call(f32[1,128,128]{2,1,0:T(8,128)S(1)} %get-tuple-element.47), custom_call_target="InvertDiagBlocksLowerTriangular" | custom-call | tf_op jit(solution)/shard_map/cholesky | solution.py:57
  363.4 11.9 %cholesky.531 = f32[128,128]{1,0:T(8,128)S(1)} custom-call(f32[128,128]{1,0:T(8,128)S(1)} %cholesky.686), custom_call_target="Cholesky" | custom-call | tf_op jit(solution)/shard_map/cholesky | solution.py:57
  376.5 9.8 %custom-call.53 = f32[1,128,128]{1,2,0:T(8,128)S(1)} custom-call(f32[1,128,128]{2,1,0:T(8,128)S(1)} %get-tuple-element.44), custom_call_target="InvertDiagBlocksLowerTriangular" | custom-call | tf_op jit(solution)/shard_map/cholesky | solution.py:57
  389.6 11.7 %cholesky.551 = f32[128,128]{1,0:T(8,128)S(1)} custom-call(f32[128,128]{1,0:T(8,128)S(1)} %cholesky.691), custom_call_target="Cholesky" | custom-call | tf_op jit(solution)/shard_map/cholesky | solution.py:57
  402.7 9.8 %custom-call.54 = f32[1,128,128]{1,2,0:T(8,128)S(1)} custom-call(f32[1,128,128]{2,1,0:T(8,128)S(1)} %get-tuple-element.41), custom_call_target="InvertDiagBlocksLowerTriangular" | custom-call | tf_op jit(solution)/shard_map/cholesky | solution.py:57
  415.5 11.9 %cholesky.571 = f32[128,128]{1,0:T(8,128)S(1)} custom-call(f32[128,128]{1,0:T(8,128)S(1)} %cholesky.696), custom_call_target="Cholesky" | custom-call | tf_op jit(solution)/shard_map/cholesky | solution.py:57
  428.8 9.8 %custom-call.55 = f32[1,128,128]{1,2,0:T(8,128)S(1)} custom-call(f32[1,128,128]{2,1,0:T(8,128)S(1)} %get-tuple-element.38), custom_call_target="InvertDiagBlocksLowerTriangular" | custom-call | tf_op jit(solution)/shard_map/cholesky | solution.py:57
  441.3 11.7 %cholesky.589 = f32[128,128]{1,0:T(8,128)S(1)} custom-call(f32[128,128]{1,0:T(8,128)S(1)} %convolution_subtract_fusion.6), custom_call_target="Cholesky" | custom-call | tf_op jit(solution)/shard_map/cholesky | solution.py:57
  464.0 5.3 %copy.32 = f32[1024,1024]{1,0:T(8,128)} copy(f32[1024,1024]{0,1:T(8,128)} %select_bitcast_fusion) | data formatting | bytes 8388608
  (106 shorter events, 99.9 us)
Async XLA Ops:
  0.6 185.8 %copy-start = (f32[1024,128]{1,0:T(8,128)S(1)}, f32[1024,128]{1,0:T(8,128)}, u32[]{:S(2)}) copy-start(f32[1024,128]{1,0:T(8,128)} %param.10) | copy-start | bytes 1572868
  0.6 5.9 %copy-start.3 = (s32[8,128]{1,0:T(8,128)S(1)}, s32[8,128]{1,0:T(8,128)}, u32[]{:S(2)}) copy-start(s32[8,128]{1,0:T(8,128)} %constant.337.clone.1) | copy-start | bytes 12292
  0.7 5.2 %copy-start.2 = (s32[16]{0:T(128)S(1)}, s32[16]{0:T(128)}, u32[]{:S(2)}) copy-start(s32[16]{0:T(128)} %param.9) | copy-start | bytes 196
  0.7 30.6 %all-to-all-start = ((bf16[4,1024,256]{2,1,0:T(8,128)(2,1)}), bf16[4,1024,256]{2,1,0:T(8,128)(2,1)S(1)}, u32[]{:S(2)}, u32[]{:S(2)}) async-start(bf16[4,1024,256]{2,1,0:T(8,128)(2,1)} %bitcast.140), calls=%async_computation | async-start | bytes 4194304 | tf_op jit(solution)/shard_map/all_to_all | solution.py:47
  91.1 38.5 %all-to-all-start.2 = ((f32[128,1,4608]{2,1,0:T(1,128)}), f32[128,1,4608]{2,1,0:T(1,128)}, u32[]{:S(2)}, u32[]{:S(2)}) async-start(f32[128,1,4608]{2,1,0:T(1,128)} %broadcast_in_dim.31), calls=%async_computation.2 | async-start | bytes 4718592 | tf_op jit(solution)/shard_map/all_to_all | solution.py:43
  159.8 2.0 copy-start.1
